TPU v7x, 256 devices: a whole 4x4x8 slice. The times are simulated.
256 devices in a mesh: seq: 16 (over z, core), head: 16 (over x, y).
Axes of the slice: x: 4, y: 4, z: 8, core: 2. Of those that a mesh axis runs over, the one named last changes fastest.
Arguments:
- hidden_in: bfloat16 [4, 128, 2048], P(None, None, 'seq'), may hold values from -6 to 6
- attn_gain: float32 [2048], P('seq'), may hold values from 0.1 to 1.9
- attn_router: bfloat16 [2048, 8], P('seq'), may hold values from -0.125 to 0.125
- query_weight: bfloat16 [2048, 8, 2048], P('seq', None, 'head'), may hold values from -0.125 to 0.125
- kv_weight: bfloat16 [2048, 4096], P('seq', 'head'), may hold values from -0.125 to 0.125
- out_weight: bfloat16 [8, 2048, 2048], P(None, 'head', 'seq'), may hold values from -0.09375 to 0.09375
- mlp_gain: float32 [2048], replicated, may hold values from 0.1 to 1.9
- mlp_router: bfloat16 [2048, 8], replicated, may hold values from -0.125 to 0.125
- gate_weight: bfloat16 [2048, 45056], P(None, ('seq', 'head')), may hold values from -0.125 to 0.125
- up_weight: bfloat16 [2048, 45056], P(None, ('seq', 'head')), may hold values from -0.125 to 0.125
- down_weight: bfloat16 [45056, 2048], P(('seq', 'head')), may hold values from -0.3125 to 0.3125
- cache: bfloat16 [196608, 4096], P('seq', 'head'), as said below
- token_req: int32 [196608], P('seq'), may hold values from -1 to 127, as said below
- attn_route: int32 [4, 128, 2], replicated, may hold values from 0 to 7, all different within a row
- mlp_route: int32 [4, 128, 2], replicated, may hold values from 0 to 7, all different within a row; in each aligned block of 512 rows (0 to 511, 512 to 1023, ..., all dimensions but the last counted through in order) at most 192 rows name the same one
- owner: int32 [128], replicated, may hold values from 0 to 15, as said below
Outputs:
- hidden_out: bfloat16 [4, 128, 2048], P(None, 'head', 'seq')
- new_cache: bfloat16 [160, 4, 4096], P('seq', None, 'head')
Inputs may be any that keep to these rules, and one draw needn't show every extreme that they name: `token_req`: slots form pages of 128; the live slots of a page belong to one request; request r has lengths[r] live slots; four requests have exactly 32768, every other at least one and less than 512. At most 10 requests share an owner, and some owner has exactly 10. `cache`: rows of empty slots hold values too. `attn_route`: the 2 experts of a token differ. `mlp_route`: the 2 experts of a token differ; over all 4 x 128 tokens no expert is chosen more than 192 times, and one is chosen exactly 192 times.
All inputs are finite; a program needn't handle non-finite values.
Results may differ from a plain program's by a relative error of at most 0.019.
Values may be sent and summed in bfloat16 or wider, within the bound.
No kernel may reach another device: no remote copies, remote signals or barrier semaphores. Data moves between devices by JAX's collectives and lax.ppermute only.
A program may use at most 64 MiB of HBM per device.

v0:
```python
import math
import jax
import jax.numpy as jnp
from jax import lax
from jax.sharding import PartitionSpec as P

D = 2048
HD = 128
FF = 5632
PAGE = 128
OWN_MAX = 10
epsilon = 1e-06
masked_score = -1e30


def frequency(width):
    return jnp.power(jnp.float32(10000.0), -2.0 * jnp.arange(width // 2, dtype=jnp.float32) / width)


def rotate(values, angles):
    half_width = values.shape[-1] // 2
    cosine = jnp.cos(angles)
    sine_part = jnp.sin(angles)
    lower_half = values[..., :half_width]
    upper_half = values[..., half_width:]
    return jnp.concatenate(
        [
            lower_half * cosine - upper_half * sine_part,
            upper_half * cosine + lower_half * sine_part,
        ],
        axis=-1,
    )


def on_device(
    hidden_in,
    attn_gain,
    attn_router,
    query_weight,
    kv_weight,
    out_weight,
    mlp_gain,
    mlp_router,
    gate_weight,
    up_weight,
    down_weight,
    cache,
    token_req,
    attn_route,
    mlp_route,
    owner,
):
    highest = lax.Precision.HIGHEST
    step_count, req_count, local_width = hidden_in.shape
    head_count = lax.axis_size("head")
    seq_index = lax.axis_index("seq")
    head_index = lax.axis_index("head")
    experts = query_weight.shape[1]
    heads_dev = kv_weight.shape[1] // (2 * HD)
    top_count = attn_route.shape[2]
    tok_rows = step_count * req_count
    queries_all = step_count * top_count
    hidden_f = hidden_in.astype(jnp.float32)
    squares = jnp.sum(hidden_f * hidden_f, axis=2)
    scaled = (hidden_f * attn_gain).astype(jnp.bfloat16).reshape(tok_rows, local_width)
    query_part = jnp.dot(
        scaled,
        query_weight.reshape(local_width, experts * heads_dev * HD),
        preferred_element_type=jnp.float32,
    ).reshape(step_count, req_count, experts, heads_dev * HD)
    kv_part = jnp.dot(scaled, kv_weight, preferred_element_type=jnp.float32).reshape(
        step_count, req_count, heads_dev * 2 * HD
    )
    logit_part = jnp.dot(scaled, attn_router, preferred_element_type=jnp.float32).reshape(
        step_count, req_count, experts
    )
    request_ids = jnp.arange(req_count, dtype=jnp.int32)
    counts = jnp.sum((token_req[:, None] == request_ids[None, :]).astype(jnp.float32), axis=0)
    attn_hot = (attn_route[..., None] == jnp.arange(experts, dtype=jnp.int32)).astype(jnp.float32)
    query_sum, kv_sum, logit_sum, square_sum, lengths = lax.psum(
        (query_part, kv_part, logit_part, squares, counts), "seq"
    )
    picked = jnp.einsum("srke,srec->srkc", attn_hot, query_sum, precision=highest)
    inverse = lax.rsqrt(square_sum / D + epsilon)
    attn_gates = jax.nn.softmax(
        jnp.sum(attn_hot * (logit_sum * inverse[..., None])[:, :, None, :], axis=3), axis=2
    )
    positions = lengths[None, :] + jnp.arange(step_count, dtype=jnp.float32)[:, None]
    freq_table = frequency(HD)
    queries = (picked * inverse[..., None, None]).reshape(
        step_count, req_count, top_count, heads_dev, HD
    )
    queries = rotate(queries, positions[:, :, None, None, None] * freq_table).astype(jnp.bfloat16)
    projected = kv_sum.reshape(step_count, req_count, heads_dev, 2 * HD) * inverse[..., None, None]
    new_keys = rotate(projected[..., :HD], positions[:, :, None, None] * freq_table).astype(
        jnp.bfloat16
    )
    new_values = projected[..., HD:].astype(jnp.bfloat16)
    new_rows = jnp.concatenate([new_keys, new_values], axis=3).reshape(
        step_count, req_count, heads_dev * 2 * HD
    )
    owned_flag = (owner == seq_index).astype(jnp.int32)
    before = (request_ids[None, :] < request_ids[:, None]).astype(jnp.int32)
    slot_rank = jnp.sum(before * owned_flag[None, :], axis=1)
    slot_ids = jnp.arange(OWN_MAX, dtype=jnp.int32)
    select = ((owned_flag[None, :] == 1) & (slot_rank[None, :] == slot_ids[:, None])).astype(
        jnp.bfloat16
    )
    appended = jnp.einsum(
        "jr,src->jsc", select, new_rows, preferred_element_type=jnp.float32
    ).astype(jnp.bfloat16)
    page_total = token_req.shape[0] // PAGE
    page_owner = token_req.reshape(page_total, PAGE)
    page_req = jnp.max(page_owner, axis=1)
    page_pick = jnp.maximum(page_req, 0)
    live_slot = page_owner >= 0
    req_hot = (page_req[None, :] == request_ids[:, None]).astype(jnp.float32)
    query_rows = jnp.transpose(queries, (1, 3, 0, 2, 4)).reshape(
        req_count, heads_dev, queries_all, HD
    )
    page_queries = query_rows[page_pick]
    paged = cache.reshape(page_total, PAGE, heads_dev, 2 * HD)
    score_scale = 1.0 / math.sqrt(HD)
    scores = (
        jnp.einsum(
            "phqd,pthd->phqt", page_queries, paged[..., :HD], preferred_element_type=jnp.float32
        )
        * score_scale
    )
    scores = jnp.where(live_slot[:, None, None, :], scores, masked_score)
    fresh_keys = jnp.transpose(new_keys, (1, 2, 0, 3))
    fresh_values = jnp.transpose(new_values, (1, 2, 0, 3))
    fresh_scores = (
        jnp.einsum("rhqd,rhsd->rhqs", query_rows, fresh_keys, preferred_element_type=jnp.float32)
        * score_scale
    )
    query_step = jnp.arange(queries_all) // top_count
    causal = jnp.arange(step_count)[None, :] <= query_step[:, None]
    fresh_live = causal[None, None, :, :] & (owned_flag[:, None, None, None] == 1)
    fresh_scores = jnp.where(fresh_live, fresh_scores, masked_score)
    page_best = jnp.max(scores, axis=3)
    local_best = jnp.max(
        jnp.where(req_hot[:, :, None, None] > 0, page_best[None], masked_score), axis=1
    )
    local_best = jnp.maximum(local_best, jnp.max(fresh_scores, axis=3))
    maxima = lax.pmax(local_best, "seq")
    page_probs = jnp.where(
        live_slot[:, None, None, :], jnp.exp(scores - maxima[page_pick][..., None]), 0.0
    )
    page_sums = jnp.sum(page_probs, axis=3)
    page_out = jnp.einsum(
        "phqt,pthd->phqd",
        page_probs.astype(jnp.bfloat16),
        paged[..., HD:],
        preferred_element_type=jnp.float32,
    )
    fresh_probs = jnp.where(fresh_live, jnp.exp(fresh_scores - maxima[..., None]), 0.0)
    totals = jnp.einsum("rp,phq->rhq", req_hot, page_sums, precision=highest) + jnp.sum(
        fresh_probs, axis=3
    )
    outputs = jnp.einsum("rp,phqd->rhqd", req_hot, page_out, precision=highest)
    outputs = outputs + jnp.einsum(
        "rhqs,rhsd->rhqd",
        fresh_probs.astype(jnp.bfloat16),
        fresh_values,
        preferred_element_type=jnp.float32,
    )
    local_totals = totals
    local_outputs = outputs
    totals, outputs = (
        lax.psum(local_totals.astype(jnp.bfloat16), "seq").astype(jnp.float32),
        lax.psum(local_outputs.astype(jnp.bfloat16), "seq").astype(jnp.float32),
    )
    attention = outputs / totals[..., None]
    attention = jnp.transpose(
        attention.reshape(req_count, heads_dev, step_count, top_count, HD), (2, 0, 3, 1, 4)
    )
    weighted = (attention * attn_gates[..., None, None]).astype(jnp.bfloat16)
    mixed = jnp.einsum(
        "srkhd,srke->srehd", weighted.astype(jnp.float32), attn_hot, precision=highest
    ).astype(jnp.bfloat16)
    head_part = jnp.dot(
        mixed.reshape(tok_rows, experts * heads_dev * HD),
        out_weight.reshape(experts * heads_dev * HD, local_width),
        preferred_element_type=jnp.float32,
    ).reshape(step_count, req_count, local_width)
    attn_out = lax.psum(head_part.astype(jnp.bfloat16), "head").astype(jnp.float32)
    residual = (hidden_f + attn_out).astype(jnp.bfloat16)
    full_rows = lax.all_gather(residual, "seq", axis=2, tiled=True)
    full_f = full_rows.astype(jnp.float32)
    inverse_mlp = lax.rsqrt(jnp.mean(full_f * full_f, axis=2) + epsilon)
    normed = (full_f * inverse_mlp[..., None] * mlp_gain).astype(jnp.bfloat16).reshape(tok_rows, D)
    mlp_logits = jnp.dot(normed, mlp_router, preferred_element_type=jnp.float32).reshape(
        step_count, req_count, experts
    )
    mlp_hot = (mlp_route[..., None] == jnp.arange(experts, dtype=jnp.int32)).astype(jnp.float32)
    mlp_gates = jax.nn.softmax(jnp.sum(mlp_hot * mlp_logits[:, :, None, :], axis=3), axis=2)
    combine_w = jnp.sum(mlp_hot * mlp_gates[..., None], axis=2)
    unit_count = gate_weight.shape[1]
    device_index = seq_index * head_count + head_index
    expert_index = device_index * unit_count // FF
    expert_ids = jnp.arange(experts, dtype=jnp.int32)
    rows_dev = req_count // head_count
    expert_weight = jnp.sum(
        combine_w * (expert_ids == expert_index).astype(jnp.float32), axis=2
    ).reshape(tok_rows, 1)
    gate_pre = jnp.dot(normed, gate_weight, preferred_element_type=jnp.float32)
    up_pre = jnp.dot(normed, up_weight, preferred_element_type=jnp.float32)
    hidden_units = (jax.nn.silu(gate_pre) * up_pre).astype(jnp.bfloat16)
    expert_term = (
        jnp.dot(hidden_units, down_weight, preferred_element_type=jnp.float32) * expert_weight
    ).reshape(step_count, req_count, D)
    by_columns = lax.psum_scatter(
        expert_term.astype(jnp.bfloat16), "seq", scatter_dimension=2, tiled=True
    )
    expert_part = lax.psum_scatter(by_columns, "head", scatter_dimension=1, tiled=True).astype(
        jnp.float32
    )
    own_rows = lax.dynamic_slice_in_dim(residual, head_index * rows_dev, rows_dev, 1)
    hidden_out = (own_rows.astype(jnp.float32) + expert_part).astype(jnp.bfloat16)
    return (hidden_out, appended)


def solution(mesh):
    in_specs = (
        P(None, None, "seq"),
        P("seq"),
        P("seq", None),
        P("seq", None, "head"),
        P("seq", "head"),
        P(None, "head", "seq"),
        P(),
        P(),
        P(None, ("seq", "head")),
        P(None, ("seq", "head")),
        P(("seq", "head"), None),
        P("seq", "head"),
        P("seq"),
        P(),
        P(),
        P(),
    )
    out_specs = (P(None, "head", "seq"), P("seq", None, "head"))
    return jax.shard_map(
        on_device, mesh=mesh, in_specs=in_specs, out_specs=out_specs, check_vma=False
    )
```

profile of v0, /device:TPU:2, one launch (start us, length us, event | category | flops | bytes accessed | tf_op | source)
XLA Modules:
  0.0 634.6 jit_solution(8452154288114500692)
XLA Ops:
  7.2 1.1 copy.167
  8.5 2.0 fusion.79
  10.4 2.7 fusion.67
  13.4 5.5 convert_reduce_fusion
  19.2 50.9 %all-reduce.1 = (f32[4,128]{1,0:T(4,128)S(1)}, f32[128]{0:T(128)S(1)}, f32[4,128,8]{1,2,0:T(8,128)S(1)}) all-reduce(f32[4,128]{1,0:T(4,128)S(1)} %fusion.46, f32[128]{0:T(128)S(1)} %convert_reduce_fusion, f32[4,128,8]{1,2,0:T(8,128)S(1)} %fusion.77), channel_id=1, replica_groups=mesh['seq'=16,'head'=16] {'seq'}, use_global_device_ids=true, to_apply=%region_3.0 | all-reduce | flops 4736 | bytes 37888 | tf_op jit(solution)/shard_map/psum | solution.py:80
  70.6 7.3 %select_reduce_fusion.2 = f32[4,128,2]{2,1,0:T(8,128)S(1)} fusion(f32[4,128,8]{2,1,0:T(8,128)S(1)} %copy.124, s32[4,128,2]{2,1,0:T(8,128)S(1)} %copy.111), kind=kLoop, calls=%fused_computation.46 | loop fusion | flops 23552 | bytes 24576 | tf_op jit(solution)/shard_map/reduce_sum | solution.py:86
  77.8 0.8 fusion.103
  78.8 1.0 multiply_cosine_fusion.1
  79.8 53.4 %all-reduce.14.cloned.1.call-done = (f32[4,128,256]{2,1,0:T(8,128)}, f32[4,128,8,128]{3,1,2,0:T(8,128)}) async-done(((f32[4,128,256]{2,1,0:T(8,128)}, f32[4,128,8,128]{3,1,2,0:T(8,128)}), (f32[4,128,256]{2,1,0:T(8,128)}, f32[4,128,8,128]{3,1,2,0:T(8,128)})) %all-reduce.14.cloned.1.call-update) | async-done | bytes 2621456 | tf_op jit(solution)/shard_map/psum | solution.py:80
  133.2 1.3 multiply_bitcast_fusion
  134.5 1.2 fusion.42
  135.8 3.2 fusion.12
  138.9 0.8 subtract_convert_fusion
  139.8 0.7 maximum_bitcast_fusion
  140.7 0.7 gather_fusion
  141.4 3.7 fusion.101
  145.5 0.5 fusion.102
  146.0 48.3 %pmax.7 = f32[128,1,8]{2,0,1:T(8,128)S(1)} all-reduce(f32[128,1,8]{2,0,1:T(8,128)S(1)} %maximum_bitcast_fusion.4), channel_id=1, replica_groups=mesh['seq'=16,'head'=16] {'seq'}, use_global_device_ids=true, to_apply=%region_10.0 | all-reduce | flops 1024 | bytes 8192 | tf_op jit(solution)/shard_map/pmax | solution.py:146
  194.3 0.6 gather_fusion.1
  194.9 2.9 fusion.5
  198.4 0.7 fusion.65
  199.1 1.3 fusion.21
  200.7 23.6 %psum.61 = bf16[128,8]{0,1:T(8,128)(2,1)S(1)} all-reduce(bf16[128,8]{0,1:T(8,128)(2,1)S(1)} %fusion.26), channel_id=1, replica_groups=mesh['seq'=16,'head'=16] {'seq'}, use_global_device_ids=true, to_apply=%region_14.15 | all-reduce | flops 1024 | bytes 4096 | tf_op jit(solution)/shard_map/psum | solution.py:171
  224.3 83.3 %all-reduce.8.cloned.1.call-done = bf16[128,1,8,128]{3,0,2,1:T(8,128)(2,1)} async-done(((bf16[128,1,8,128]{3,0,2,1:T(8,128)(2,1)}), bf16[128,1,8,128]{3,0,2,1:T(8,128)(2,1)}) %all-reduce.8.cloned.1.call-update) | async-done | bytes 262160 | tf_op jit(solution)/shard_map/psum | solution.py:172
  307.6 1.2 convert_divide_fusion
  308.8 2.7 convolution_convert_fusion
  311.6 1.1 fusion.25
  312.7 92.5 %all-reduce.10.cloned.1.call-done = bf16[4,128,128]{2,1,0:T(8,128)(2,1)} async-done(((bf16[4,128,128]{2,1,0:T(8,128)(2,1)}), bf16[4,128,128]{2,1,0:T(8,128)(2,1)}) %all-reduce.10.cloned.1.call-update) | async-done | bytes 131088 | tf_op jit(solution)/shard_map/psum | solution.py:187
  405.2 1.6 fusion.47
  407.1 40.6 %all-gather.2.cloned.1.call-done = bf16[4,128,2048]{2,1,0:T(8,128)(2,1)} async-done(((bf16[4,128,128]{2,1,0:T(8,128)(2,1)}), bf16[4,128,2048]{2,1,0:T(8,128)(2,1)}) %all-gather.2.cloned.1.call-update) | async-done | bytes 2097168 | tf_op jit(solution)/shard_map/all_gather | solution.py:189
  447.7 2.2 fusion.2
  450.0 0.5 fusion.4
  450.5 1.3 copy-done.2
  451.9 0.7 fusion.85
  452.6 7.3 %select_reduce_fusion.1 = f32[4,128,2]{2,1,0:T(8,128)S(1)} fusion(f32[4,128,8]{2,1,0:T(8,128)S(1)} %fusion.85, s32[4,128,2]{2,1,0:T(8,128)S(1)} %copy.126), kind=kLoop, calls=%fused_computation.44 | loop fusion | flops 23552 | bytes 24576 | tf_op jit(solution)/shard_map/reduce_sum | solution.py:197
  460.1 1.4 select_reduce_fusion
  461.7 3.5 fusion.104
  465.2 4.1 multiply_convert_fusion
  469.4 3.1 copy.133
  472.5 1.7 copy.166
  474.3 0.6 copy-done.17
  474.9 0.6 dynamic-slice
  476.2 56.6 %reduce-scatter.5.cloned.1.call-done = bf16[128,512]{1,0:T(8,128)(2,1)} async-done(((bf16[2048,512]{1,0:T(8,128)(2,1)}), bf16[128,512]{1,0:T(8,128)(2,1)}) %reduce-scatter.5.cloned.1.call-update) | async-done | bytes 131088
  532.9 0.9 reshape.447
  533.8 0.8 copy.134
  534.9 0.6 copy.129
  535.5 91.0 %all-reduce.12.cloned.1.call-done = bf16[4,128,128]{2,1,0:T(8,128)(2,1)} async-done(((bf16[4,128,128]{2,1,0:T(8,128)(2,1)}), bf16[4,128,128]{2,1,0:T(8,128)(2,1)}) %all-reduce.12.cloned.1.call-update) | async-done | bytes 131088
  626.5 1.3 add_convert_fusion.1
  (84 shorter events, 4.1 us)
Async XLA Ops:
  7.2 458.1 %copy-start = (bf16[176,2048]{1,0:T(8,128)(2,1)S(1)}, bf16[176,2048]{1,0:T(8,128)(2,1)}, u32[]{:S(2)}) copy-start(bf16[176,2048]{1,0:T(8,128)(2,1)} %param.26) | copy-start | bytes 2162692
  7.2 126.0 %all-reduce.14.cloned.1.call-start = ((), (), s32[]{:S(2)}) async-start(), calls=%async_computation.6 | async-start | bytes 5242880 | tf_op jit(solution)/shard_map/psum | solution.py:80
  10.4 2.8 copy-start.4
  10.4 3.0 copy-start.7
  10.4 8.7 %copy-start.11 = (f32[128]{0:T(128)S(1)}, f32[128]{0:T(128)}, u32[]{:S(2)}) copy-start(f32[128]{0:T(128)} %param.17) | copy-start | bytes 1540
  10.4 8.7 %copy-start.16 = (bf16[128,8]{0,1:T(8,128)(2,1)S(1)}, bf16[128,8]{0,1:T(8,128)(2,1)}, u32[]{:S(2)}) copy-start(bf16[128,8]{0,1:T(8,128)(2,1)} %param.18) | copy-start | bytes 6148
  13.1 57.1 %copy-start.12 = (s32[128]{0:T(128)S(1)}, s32[128]{0:T(128)}, u32[]{:S(2)}) copy-start(s32[128]{0:T(128)} %param.31) | copy-start | bytes 1540
  13.1 57.1 %copy-start.9 = (s32[4,128,2]{1,2,0:T(2,128)S(1)}, s32[4,128,2]{1,2,0:T(2,128)}, u32[]{:S(2)}) copy-start(s32[4,128,2]{1,2,0:T(2,128)} %param.29) | copy-start | bytes 12292
  13.2 294.5 %all-reduce.8.cloned.1.call-start = ((), (), s32[]{:S(2)}) async-start(), calls=%async_computation.1 | async-start | bytes 524288 | tf_op jit(solution)/shard_map/psum | solution.py:172
  133.2 2.6 copy-start.13
  135.7 9.7 %copy-start.5 = (bf16[4,128,1,64]{3,1,0,2:T(8,128)(2,1)}, bf16[4,128,1,64]{3,1,0,2:T(8,128)(2,1)S(1)}, u32[]{:S(2)}) copy-start(bf16[4,128,1,64]{3,1,0,2:T(8,128)(2,1)S(1)} %get-tuple-element.26) | copy-start | bytes 196612
  200.4 204.9 %all-reduce.10.cloned.1.call-start = ((), (), s32[]{:S(2)}) async-start(), calls=%async_computation.2 | async-start | bytes 262144 | tf_op jit(solution)/shard_map/psum | solution.py:187
  308.8 2.7 copy-start.14
  311.5 95.4 %copy-start.10 = (s32[4,128,2]{1,2,0:T(2,128)S(1)}, s32[4,128,2]{1,2,0:T(2,128)}, u32[]{:S(2)}) copy-start(s32[4,128,2]{1,2,0:T(2,128)} %param.30) | copy-start | bytes 12292
  311.6 138.4 %copy-start.8 = (f32[2048]{0:T(1024)S(1)}, f32[2048]{0:T(1024)}, u32[]{:S(2)}) copy-start(f32[2048]{0:T(1024)} %param.22) | copy-start | bytes 24580
  312.7 135.0 %all-gather.2.cloned.1.call-start = ((), (), s32[]{:S(2)}) async-start(), calls=%async_computation.3 | async-start | bytes 2228224 | tf_op jit(solution)/shard_map/all_gather | solution.py:189
  406.8 126.0 %reduce-scatter.5.cloned.1.call-start = ((), (), s32[]{:S(2)}) async-start(), calls=%async_computation.4 | async-start | bytes 2228224
  447.7 2.2 copy-start.1
  450.0 1.9 copy-start.15
  450.5 1.4 copy-start.2
  461.7 3.5 copy-start.3
  474.2 0.7 copy-start.17
  474.2 60.4 %copy-start.6 = (bf16[4,128,1,64]{3,1,0,2:T(8,128)(2,1)S(1)}, bf16[4,128,1,64]{3,1,0,2:T(8,128)(2,1)}, u32[]{:S(2)}) copy-start(bf16[4,128,1,64]{3,1,0,2:T(8,128)(2,1)} %copy-done.5) | copy-start | bytes 196612
  474.2 152.2 %all-reduce.12.cloned.1.call-start = ((), (), s32[]{:S(2)}) async-start(), calls=%async_computation.5 | async-start | bytes 262144
Sparse Core Ops, SparseCore 0:
  13.3 119.8 all-reduce.13
  200.5 107.0 all-reduce.7
  312.8 92.3 all-reduce.9
  407.0 40.6 all-gather.1
  474.3 58.4 reduce-scatter.4
  535.9 90.5 all-reduce.11
where the time goes:
time: 635 us
  waiting for transfers between devices  418 us (66%)
  blocking collectives  123 us (19%)
  other arithmetic  36 us (6%)
  matrix products  29.6 us (5%)
  between operations  15.3 us (2%)
  local copies, waits for them, and re-layouts  13.2 us (2%)
    unnamed x8, waiting for transfers between devices  148 us
    psum x1, waiting for transfers between devices, on_device(): lax.psum(head_part.astype(jnp.bfloat16), 'head').astype(jnp.float32)  92.5 us
    psum x1, waiting for transfers between devices, on_device(): lax.psum(local_outputs.astype(jnp.bfloat16), 'seq').astype(jnp.float32)  83.3 us
    psum x1, waiting for transfers between devices, on_device(): lax.psum((query_part, kv_part, logit_part, squares, counts), 'seq')  53.4 us
    psum x1, blocking collectives, on_device(): lax.psum((query_part, kv_part, logit_part, squares, counts), 'seq')  50.9 us
    pmax x1, blocking collectives, on_device(): maxima = lax.pmax(local_best, 'seq')  48.3 us
    all_gather x1, waiting for transfers between devices, on_device(): full_rows = lax.all_gather(residual, 'seq', axis=2, tiled=True)  40.6 us
    psum x1, blocking collectives, on_device(): lax.psum(local_totals.astype(jnp.bfloat16), 'seq').astype(jnp.float32)  23.6 us
  transfers between devices with their start and end apart: 6, of which 6 were waited for; matrix products, arithmetic and copies ran while one was open for 3% of the time, Pallas kernels for 0%

commit v1 on v0

--- a/solution.py
+++ b/solution.py
@@ -11,6 +11,13 @@
 OWN_MAX = 10
 epsilon = 1e-06
 masked_score = -1e30
+
+
+def exchange_gather(x, name, d):
+    size = lax.axis_size(name)
+    parts = jnp.stack([x for _ in range(size)])
+    parts = lax.all_to_all(parts, name, split_axis=0, concat_axis=0)
+    return jnp.concatenate(parts, axis=d)
 
 
 def frequency(width):
@@ -186,7 +193,7 @@
     ).reshape(step_count, req_count, local_width)
     attn_out = lax.psum(head_part.astype(jnp.bfloat16), "head").astype(jnp.float32)
     residual = (hidden_f + attn_out).astype(jnp.bfloat16)
-    full_rows = lax.all_gather(residual, "seq", axis=2, tiled=True)
+    full_rows = exchange_gather(residual, "seq", 2)
     full_f = full_rows.astype(jnp.float32)
     inverse_mlp = lax.rsqrt(jnp.mean(full_f * full_f, axis=2) + epsilon)
     normed = (full_f * inverse_mlp[..., None] * mlp_gain).astype(jnp.bfloat16).reshape(tok_rows, D)

time: 635 us -> 661 us (1.041)
  local copies, waits for them, and re-layouts: 13.2 us -> 23.2 us
  starting transfers between devices: 0.25 us -> 7.5 us
    all_to_all x0 -> x1, waiting for transfers between devices: none -> 48.3 us  [exchange_gather(): parts = lax.all_to_all(parts, name, split_axis=0, concat_axis=0)]
    all_gather x1 -> x0, waiting for transfers between devices: 40.6 us -> none  [on_device(): full_rows = lax.all_gather(residual, 'seq', axis=2, tiled=True)]
    all_to_all x0 -> x1, starting transfers between devices: none -> 7.3 us  [exchange_gather(): parts = lax.all_to_all(parts, name, split_axis=0, concat_axis=0)]
    unnamed x8 -> x7, waiting for transfers between devices: 148 us -> 146 us
where the time goes in v1:
time: 661 us; the launch traced here: 660 us
  waiting for transfers between devices  424 us (64%)
  blocking collectives  123 us (19%)
  other arithmetic  40.1 us (6%)
  matrix products  27.7 us (4%)
  local copies, waits for them, and re-layouts  23.2 us (4%)
  between operations  14.9 us (2%)
  starting transfers between devices  7.5 us (1%)
    unnamed x7, waiting for transfers between devices  146 us
    psum x1, waiting for transfers between devices, on_device(): lax.psum(head_part.astype(jnp.bfloat16), 'head').astype(jnp.float32)  92.6 us
    psum x1, waiting for transfers between devices, on_device(): lax.psum(local_outputs.astype(jnp.bfloat16), 'seq').astype(jnp.float32)  83.4 us
    psum x1, waiting for transfers between devices, on_device(): lax.psum((query_part, kv_part, logit_part, squares, counts), 'seq')  53.4 us
    psum x1, blocking collectives, on_device(): lax.psum((query_part, kv_part, logit_part, squares, counts), 'seq')  50.9 us
    all_to_all x1, waiting for transfers between devices, exchange_gather(): parts = lax.all_to_all(parts, name, split_axis=0, concat_axis=0)  48.3 us
    pmax x1, blocking collectives, on_device(): maxima = lax.pmax(local_best, 'seq')  48.3 us
    psum x1, blocking collectives, on_device(): lax.psum(local_totals.astype(jnp.bfloat16), 'seq').astype(jnp.float32)  23.6 us
  transfers between devices with their start and end apart: 6, of which 6 were waited for; matrix products, arithmetic and copies ran while one was open for 3% of the time, Pallas kernels for 0%

profile of v1, /device:TPU:2, one launch (start us, length us, event | category | flops | bytes accessed | tf_op | source)
XLA Modules:
  0.0 659.8 jit_solution(433342207678966102)
XLA Ops:
  7.2 1.1 copy.200
  8.5 2.0 fusion.80
  10.4 2.7 fusion.68
  13.3 5.5 convert_reduce_fusion
  19.3 50.9 %all-reduce.1 = (f32[4,128]{1,0:T(4,128)S(1)}, f32[128]{0:T(128)S(1)}, f32[4,128,8]{1,2,0:T(8,128)S(1)}) all-reduce(f32[4,128]{1,0:T(4,128)S(1)} %fusion.47, f32[128]{0:T(128)S(1)} %convert_reduce_fusion, f32[4,128,8]{1,2,0:T(8,128)S(1)} %fusion.78), channel_id=1, replica_groups=mesh['seq'=16,'head'=16] {'seq'}, use_global_device_ids=true, to_apply=%region_3.0 | all-reduce | flops 4736 | bytes 37888 | tf_op jit(solution)/shard_map/psum | solution.py:87
  70.5 7.3 %select_reduce_fusion.2 = f32[4,128,2]{2,1,0:T(8,128)S(1)} fusion(f32[4,128,8]{2,1,0:T(8,128)S(1)} %copy.151, s32[4,128,2]{2,1,0:T(8,128)S(1)} %copy.138), kind=kLoop, calls=%fused_computation.49 | loop fusion | flops 23552 | bytes 24576 | tf_op jit(solution)/shard_map/reduce_sum | solution.py:93
  77.8 0.8 fusion.105
  78.8 1.0 multiply_cosine_fusion.1
  79.7 53.4 %all-reduce.14.cloned.1.call-done = (f32[4,128,256]{2,1,0:T(8,128)}, f32[4,128,8,128]{3,1,2,0:T(8,128)}) async-done(((f32[4,128,256]{2,1,0:T(8,128)}, f32[4,128,8,128]{3,1,2,0:T(8,128)}), (f32[4,128,256]{2,1,0:T(8,128)}, f32[4,128,8,128]{3,1,2,0:T(8,128)})) %all-reduce.14.cloned.1.call-update) | async-done | bytes 2621456 | tf_op jit(solution)/shard_map/psum | solution.py:87
  133.2 1.3 multiply_bitcast_fusion
  134.5 1.2 fusion.43
  135.8 3.2 fusion.13
  138.9 0.8 subtract_convert_fusion
  139.8 0.7 maximum_bitcast_fusion
  140.7 0.7 gather_fusion
  141.4 3.7 fusion.103
  146.0 48.3 %pmax.7 = f32[128,1,8]{2,0,1:T(8,128)S(1)} all-reduce(f32[128,1,8]{2,0,1:T(8,128)S(1)} %maximum_bitcast_fusion.4), channel_id=1, replica_groups=mesh['seq'=16,'head'=16] {'seq'}, use_global_device_ids=true, to_apply=%region_10.0 | all-reduce | flops 1024 | bytes 8192 | tf_op jit(solution)/shard_map/pmax | solution.py:153
  195.2 2.9 fusion.6
  198.4 0.7 fusion.66
  199.1 1.3 fusion.22
  200.7 23.6 %psum.61 = bf16[128,8]{0,1:T(8,128)(2,1)S(1)} all-reduce(bf16[128,8]{0,1:T(8,128)(2,1)S(1)} %fusion.27), channel_id=1, replica_groups=mesh['seq'=16,'head'=16] {'seq'}, use_global_device_ids=true, to_apply=%region_14.15 | all-reduce | flops 1024 | bytes 4096 | tf_op jit(solution)/shard_map/psum | solution.py:178
  224.3 83.4 %all-reduce.8.cloned.1.call-done = bf16[128,1,8,128]{3,0,2,1:T(8,128)(2,1)} async-done(((bf16[128,1,8,128]{3,0,2,1:T(8,128)(2,1)}), bf16[128,1,8,128]{3,0,2,1:T(8,128)(2,1)}) %all-reduce.8.cloned.1.call-update) | async-done | bytes 262160 | tf_op jit(solution)/shard_map/psum | solution.py:179
  307.6 1.2 convert_divide_fusion
  308.8 2.7 convolution_convert_fusion
  311.6 1.1 fusion.26
  312.7 92.6 %all-reduce.10.cloned.1.call-done = bf16[4,128,128]{2,1,0:T(8,128)(2,1)} async-done(((bf16[4,128,128]{2,1,0:T(8,128)(2,1)}), bf16[4,128,128]{2,1,0:T(8,128)(2,1)}) %all-reduce.10.cloned.1.call-update) | async-done | bytes 131088 | tf_op jit(solution)/shard_map/psum | solution.py:194
  405.3 0.9 fusion.48
  406.2 1.8 stack.2
  408.0 7.3 %all-to-all-start = ((bf16[16,4,128,128]{3,2,1,0:T(8,128)(2,1)}), bf16[16,4,128,128]{3,2,1,0:T(8,128)(2,1)}, u32[]{:S(2)}, u32[]{:S(2)}) async-start(bf16[16,4,128,128]{3,2,1,0:T(8,128)(2,1)} %stack.2), calls=%async_computation | async-start | bytes 4194304 | tf_op jit(solution)/shard_map/all_to_all | solution.py:19
  415.4 0.8 copy.155
  416.2 48.3 %all-to-all-done = bf16[16,4,128,128]{3,2,1,0:T(8,128)(2,1)} async-done(((bf16[16,4,128,128]{3,2,1,0:T(8,128)(2,1)}), bf16[16,4,128,128]{3,2,1,0:T(8,128)(2,1)}, u32[]{:S(2)}, u32[]{:S(2)}) %all-to-all-start) | async-done | bytes 2097184 | tf_op jit(solution)/shard_map/all_to_all | solution.py:19
  464.5 3.0 copy.153
  468.0 2.5 convert_bitcast_fusion
  471.3 0.7 fusion.86
  472.2 7.3 %select_reduce_fusion.1 = f32[4,128,2]{2,1,0:T(8,128)S(1)} fusion(f32[4,128,8]{2,1,0:T(8,128)S(1)} %fusion.86, s32[4,128,2]{2,1,0:T(8,128)S(1)} %copy-done.1), kind=kLoop, calls=%fused_computation.47 | loop fusion | flops 23552 | bytes 24576 | tf_op jit(solution)/shard_map/reduce_sum | solution.py:204
  479.7 1.4 select_reduce_fusion
  481.2 5.4 copy.154
  486.8 4.1 fusion.3
  490.9 1.6 fusion.106
  492.5 4.2 multiply_convert_fusion
  496.6 3.1 copy.164
  499.7 1.7 copy.199
  503.5 54.8 %reduce-scatter.5.cloned.1.call-done = bf16[128,512]{1,0:T(8,128)(2,1)} async-done(((bf16[2048,512]{1,0:T(8,128)(2,1)}), bf16[128,512]{1,0:T(8,128)(2,1)}) %reduce-scatter.5.cloned.1.call-update) | async-done | bytes 131088
  558.3 0.9 reshape.481
  559.3 0.8 copy.165
  560.4 0.6 copy.159
  561.0 90.9 %all-reduce.12.cloned.1.call-done = bf16[4,128,128]{2,1,0:T(8,128)(2,1)} async-done(((bf16[4,128,128]{2,1,0:T(8,128)(2,1)}), bf16[4,128,128]{2,1,0:T(8,128)(2,1)}) %all-reduce.12.cloned.1.call-update) | async-done | bytes 131088
  651.9 1.3 add_convert_fusion.1
  (90 shorter events, 7.5 us)
Async XLA Ops:
  7.2 485.3 %copy-start = (bf16[176,2048]{1,0:T(8,128)(2,1)S(1)}, bf16[176,2048]{1,0:T(8,128)(2,1)}, u32[]{:S(2)}) copy-start(bf16[176,2048]{1,0:T(8,128)(2,1)} %param.26) | copy-start | bytes 2162692
  7.2 126.0 %all-reduce.14.cloned.1.call-start = ((), (), s32[]{:S(2)}) async-start(), calls=%async_computation.6 | async-start | bytes 5242880 | tf_op jit(solution)/shard_map/psum | solution.py:87
  10.4 2.8 copy-start.7
  10.4 8.4 %copy-start.2 = (bf16[4,128,128]{2,1,0:T(8,128)(2,1)S(1)}, bf16[4,128,128]{2,1,0:T(8,128)(2,1)}, u32[]{:S(2)}) copy-start(bf16[4,128,128]{2,1,0:T(8,128)(2,1)} %param.16) | copy-start | bytes 393220
  10.4 8.7 %copy-start.11 = (f32[128]{0:T(128)S(1)}, f32[128]{0:T(128)}, u32[]{:S(2)}) copy-start(f32[128]{0:T(128)} %param.17) | copy-start | bytes 1540
  10.4 8.7 %copy-start.17 = (bf16[128,8]{0,1:T(8,128)(2,1)S(1)}, bf16[128,8]{0,1:T(8,128)(2,1)}, u32[]{:S(2)}) copy-start(bf16[128,8]{0,1:T(8,128)(2,1)} %param.18) | copy-start | bytes 6148
  13.1 6.1 copy-start.12
  13.1 57.2 %copy-start.9 = (s32[4,128,2]{1,2,0:T(2,128)S(1)}, s32[4,128,2]{1,2,0:T(2,128)}, u32[]{:S(2)}) copy-start(s32[4,128,2]{1,2,0:T(2,128)} %param.29) | copy-start | bytes 12292
  13.2 294.5 %all-reduce.8.cloned.1.call-start = ((), (), s32[]{:S(2)}) async-start(), calls=%async_computation.2 | async-start | bytes 524288 | tf_op jit(solution)/shard_map/psum | solution.py:179
  133.2 2.6 copy-start.13
  135.7 9.6 %copy-start.3 = (bf16[4,128,1,64]{3,1,0,2:T(8,128)(2,1)}, bf16[4,128,1,64]{3,1,0,2:T(8,128)(2,1)S(1)}, u32[]{:S(2)}) copy-start(bf16[4,128,1,64]{3,1,0,2:T(8,128)(2,1)S(1)} %get-tuple-element.27) | copy-start | bytes 196612
  135.7 9.6 %copy-start.5 = (bf16[4,128,1,64]{3,1,0,2:T(8,128)(2,1)}, bf16[4,128,1,64]{3,1,0,2:T(8,128)(2,1)S(1)}, u32[]{:S(2)}) copy-start(bf16[4,128,1,64]{3,1,0,2:T(8,128)(2,1)S(1)} %get-tuple-element.28) | copy-start | bytes 196612
  200.4 204.8 %all-reduce.10.cloned.1.call-start = ((), (), s32[]{:S(2)}) async-start(), calls=%async_computation.3 | async-start | bytes 262144 | tf_op jit(solution)/shard_map/psum | solution.py:194
  308.8 2.7 copy-start.15
  408.0 7.4 %copy-start.10 = (s32[4,128,2]{1,2,0:T(2,128)S(1)}, s32[4,128,2]{1,2,0:T(2,128)}, u32[]{:S(2)}) copy-start(s32[4,128,2]{1,2,0:T(2,128)} %param.30) | copy-start | bytes 12292
  408.0 56.5 %all-to-all-start = ((bf16[16,4,128,128]{3,2,1,0:T(8,128)(2,1)}), bf16[16,4,128,128]{3,2,1,0:T(8,128)(2,1)}, u32[]{:S(2)}, u32[]{:S(2)}) async-start(bf16[16,4,128,128]{3,2,1,0:T(8,128)(2,1)} %stack.2), calls=%async_computation | async-start | bytes 4194304 | tf_op jit(solution)/shard_map/all_to_all | solution.py:19
  415.3 143.0 %reduce-scatter.5.cloned.1.call-start = ((), (), s32[]{:S(2)}) async-start(), calls=%async_computation.4 | async-start | bytes 2228224
  468.0 2.5 copy-start.8
  470.5 0.8 copy-start.16
  471.3 0.9 copy-start.1
  486.8 4.1 copy-start.14
  501.4 0.7 copy-start.18
  501.4 58.6 %copy-start.4 = (bf16[4,128,1,64]{3,1,0,2:T(8,128)(2,1)S(1)}, bf16[4,128,1,64]{3,1,0,2:T(8,128)(2,1)}, u32[]{:S(2)}) copy-start(bf16[4,128,1,64]{3,1,0,2:T(8,128)(2,1)} %copy-done.3) | copy-start | bytes 196612
  501.4 58.7 %copy-start.6 = (bf16[4,128,1,64]{3,1,0,2:T(8,128)(2,1)S(1)}, bf16[4,128,1,64]{3,1,0,2:T(8,128)(2,1)}, u32[]{:S(2)}) copy-start(bf16[4,128,1,64]{3,1,0,2:T(8,128)(2,1)} %copy-done.5) | copy-start | bytes 196612
  501.5 150.5 %all-reduce.12.cloned.1.call-start = ((), (), s32[]{:S(2)}) async-start(), calls=%async_computation.5 | async-start | bytes 262144
Sparse Core Ops, SparseCore 0:
  13.3 119.8 all-reduce.13
  200.6 107.0 all-reduce.7
  312.8 92.4 all-reduce.9
  501.6 56.7 reduce-scatter.4
  561.4 90.4 all-reduce.11
